TPU v7x, 128 devices: a whole 4x4x4 slice. The times are simulated.
128 devices in a mesh: req: 8 (over y, core), voc: 16 (over x, z).
Axes of the slice: x: 4, y: 4, z: 4, core: 2. Of those that a mesh axis runs over, the one named last changes fastest.
Arguments:
- hidden: bfloat16 [16384, 1536], P(('req', 'voc')), may hold values from -64 to 64
- norm_gain: float32 [1536], replicated, may hold values from 0.1 to 1.9
- head: bfloat16 [1536, 49152], P(None, 'voc'), may hold values from -8 to 8
- targets: int32 [16384], P(('req', 'voc')), may hold values from 0 to 49151
- bounds: int32 [128, 2], P(('req', 'voc')), may hold values from 0 to 128, as said below
Outputs:
- logprob: float32 [16384], P(('req', 'voc'))
- entropy: float32 [16384], P(('req', 'voc'))
- target_logit: float32 [16384], P(('req', 'voc'))
- mean_entropy: float32 [1], replicated
Inputs may be any that keep to these rules, and one draw needn't show every extreme that they name: bounds[d] = (lo, hi): slots lo to hi - 1 of device d hold live response rows; 1 <= hi - lo <= 96, lo <= 32; some device has hi - lo = 96 and hi = 128, some has lo = 0.
All inputs are finite; a program needn't handle non-finite values.
Results may differ from a plain program's by a relative error of at most 0.00075.
The roundings to bfloat16 on the way count: a program that leaves them out, or rounds other values in their place, can miss the bound.
Values may be sent and summed in bfloat16 or wider, within the bound.
No kernel may reach another device: no remote copies, remote signals or barrier semaphores. Data moves between devices by JAX's collectives and lax.ppermute only.
A program may use at most 64 MiB of HBM per device.

v0:
```python
import jax
import jax.numpy as jnp
from jax import lax
from jax.sharding import PartitionSpec as P

LIVE = 96
CHUNK = 32


def pick_block(count):
    size = min(count, 512)
    while count % size:
        size -= 1
    return size


def combine_stats(first, second):
    top = jnp.maximum(first[0], second[0])
    weight_a = jnp.exp(first[0] - top)
    weight_b = jnp.exp(second[0] - top)
    return jnp.stack(
        [
            top,
            first[1] * weight_a + second[1] * weight_b,
            first[2] * weight_a + second[2] * weight_b,
            first[3] + second[3],
        ]
    )


def butterfly(value, axis, combine):
    size = lax.axis_size(axis)
    index = lax.axis_index(axis)
    step = 1
    while step < size:
        other = lax.ppermute(value, axis, [(i, i ^ step) for i in range(size)])
        upper = index & step != 0
        first = jnp.where(upper, other, value)
        second = jnp.where(upper, value, other)
        value = combine(first, second)
        step *= 2
    return value


def members(value, axis, sub, stride):
    size = lax.axis_size(axis)
    digit = lax.axis_index(axis) // stride % sub
    received = [value]
    for shift in range(1, sub):
        pairs = []
        for i in range(size):
            d = i // stride % sub
            pairs.append((i, i + ((d + shift) % sub - d) * stride))
        received.append(lax.ppermute(value, axis, pairs))
    order = (digit - jnp.arange(sub, dtype=jnp.int32)) % sub
    return jnp.take(jnp.stack(received), order, axis=0)


def tree(items, combine):
    items = list(items)
    while len(items) > 1:
        items = [combine(items[i], items[i + 1]) for i in range(0, len(items), 2)]
    return items[0]


def shard_stats(gathered, local_ids, head):
    count = gathered.shape[0]
    width = gathered.shape[1]
    block = pick_block(count)
    columns = jnp.arange(head.shape[1], dtype=jnp.int32)

    def one_block(pair):
        rows_in, ids = pair
        logits = jnp.dot(rows_in, head, preferred_element_type=jnp.float32)
        top = jnp.max(logits, axis=-1)
        expo = jnp.exp(logits - top[:, None])
        total = jnp.sum(expo, axis=-1)
        weighted = jnp.sum(expo * logits, axis=-1)
        picked = jnp.sum(jnp.where(columns[None, :] == ids[:, None], logits, 0.0), axis=-1)
        return jnp.stack([top, total, weighted, picked])

    outputs = lax.map(
        one_block,
        (gathered.reshape(count // block, block, width), local_ids.reshape(count // block, block)),
    )
    return jnp.transpose(outputs, (1, 0, 2)).reshape(4, count)


def shards(hidden, norm_gain, head, targets, bounds):
    slots = hidden.shape[0]
    shard_width = head.shape[1]
    groups = lax.axis_size("voc")
    position = lax.axis_index("voc")
    start = bounds[0, 0]
    finish = bounds[0, 1]
    live_count = finish - start
    rows = lax.dynamic_slice_in_dim(hidden, start, LIVE, 0)
    values = rows.astype(jnp.float32)
    meansq = jnp.mean(values * values, axis=-1, keepdims=True)
    normed = (values * lax.rsqrt(meansq + 1e-05) * norm_gain).astype(jnp.bfloat16)
    ids = lax.dynamic_slice_in_dim(targets, start, LIVE, 0)
    meta = jnp.concatenate([ids, jnp.full((8,), live_count, jnp.int32)])
    gathered_meta = lax.all_gather(meta, "voc", axis=0)
    gathered_ids = gathered_meta[:, :LIVE]
    counts = gathered_meta[:, LIVE]
    local_ids = gathered_ids - position * shard_width
    parts = []
    for first in range(0, LIVE, CHUNK):
        gathered = lax.all_gather(normed[first : first + CHUNK], "voc", axis=0, tiled=True)
        part = shard_stats(gathered, local_ids[:, first : first + CHUNK].reshape(-1), head)
        parts.append(part.reshape(4, groups, CHUNK))
    stats = jnp.stack(parts, axis=2).reshape(4, groups * LIVE)
    inner = 4 if groups % 4 == 0 else 1
    merged = stats
    if inner > 1:
        merged = tree(members(merged, "voc", inner, 1), combine_stats)
    merged = tree(members(merged, "voc", groups // inner, inner), combine_stats)
    top, total, weighted, picked = (merged[0], merged[1], merged[2], merged[3])
    lse = top + jnp.log(total)
    row_entropy = lse - weighted / total
    row_logprob = picked - lse
    slot = jnp.arange(LIVE, dtype=jnp.int32)
    group_live = slot[None, :] < counts[:, None]
    group_entropy = jnp.where(group_live, row_entropy.reshape(groups, LIVE), 0.0)
    totals = jnp.stack([jnp.sum(group_entropy), jnp.sum(counts).astype(jnp.float32)])
    totals = tree(members(totals, "req", lax.axis_size("req"), 1), lambda a, b: a + b)
    mean_entropy = (totals[0] / totals[1]).reshape(1)
    own = lambda a: lax.dynamic_slice_in_dim(a, position * LIVE, LIVE, 0)
    live = slot < live_count
    zero = jnp.zeros((LIVE,), jnp.float32)
    place = lambda a: lax.dynamic_update_slice_in_dim(jnp.zeros((slots,), jnp.float32), a, start, 0)
    entropy = place(jnp.where(live, own(row_entropy), zero))
    logprob = place(jnp.where(live, own(row_logprob), zero))
    target_logit = place(jnp.where(live, own(picked), zero))
    return (logprob, entropy, target_logit, mean_entropy)


def solution(mesh):
    placed = (
        P(("req", "voc"), None),
        P(),
        P(None, "voc"),
        P(("req", "voc")),
        P(("req", "voc"), None),
    )
    return jax.shard_map(
        shards,
        mesh=mesh,
        in_specs=placed,
        out_specs=(P(("req", "voc")), P(("req", "voc")), P(("req", "voc")), P()),
        check_vma=False,
    )
```

profile of v0, /device:TPU:1, one launch (start us, length us, event | category | flops | bytes accessed | tf_op | source)
XLA Modules:
  0.0 206.2 jit_solution(10489201134984408602)
XLA Ops:
  7.2 1.3 fusion.51
  10.5 1.2 fusion.3
  11.7 1.1 fusion.5
  12.8 0.7 fusion.48
  13.6 0.7 all-gather.7.cloned.1.call-update
  14.3 0.7 all-gather.9.cloned.1.call-update
  15.1 0.7 dynamic_slice.32
  17.1 1.2 dynamic-slice.4
  19.1 14.9 %all-reduce.1 = s32[1664]{0:T(1024)S(1)} all-reduce(s32[1664]{0:T(1024)S(1)} %pad_dynamic-update-slice_fusion), channel_id=2, replica_groups=mesh['req'=8,'voc'=16] {'voc'}, use_global_device_ids=true, to_apply=%add.1 | all-reduce | flops 1664 | bytes 13312
  34.1 0.7 slice_reduce_fusion.1
  35.3 24.1 %all-gather.5.cloned.1.call-done = bf16[512,1536]{1,0:T(8,128)(2,1)} async-done(((bf16[32,1536]{1,0:T(8,128)(2,1)}), bf16[512,1536]{1,0:T(8,128)(2,1)}) %all-gather.5.cloned.1.call-update) | async-done | bytes 1572880 | tf_op jit(solution)/shard_map/all_gather | solution.py:109
  59.5 9.8 %fusion.54 = (f32[512]{0:T(512)S(1)}, f32[512,3072]{1,0:T(8,128)}) fusion(bf16[512,1536]{1,0:T(8,128)(2,1)} %all-gather.5.cloned.1.call-done, bf16[1536,3072]{1,0:T(8,128)(2,1)} %param.9), kind=kOutput, calls=%fused_computation.162 | convolution fusion | flops 4833410560 | bytes 17303552 | tf_op jit(solution)/shard_map/while/body/eval_jaxpr/dot_general | solution.py:74
  69.4 4.6 %fusion.2 = (f32[512]{0:T(512)S(1)}, f32[512]{0:T(512)S(1)}, f32[512]{0:T(512)S(1)}) fusion(f32[512,3072]{1,0:T(8,128)} %get-tuple-element.117, f32[512]{0:T(512)S(1)} %get-tuple-element.116, s32[512]{0:T(512)S(1)} %eq.76), kind=kLoop, calls=%fused_computation.17 | loop fusion | flops 11008512 | bytes 6301696 | tf_op jit(solution)/shard_map/while/body/eval_jaxpr/reduce_sum | solution.py:77
  74.3 30.5 %all-gather.7.cloned.1.call-done = bf16[512,1536]{1,0:T(8,128)(2,1)} async-done(((bf16[32,1536]{1,0:T(8,128)(2,1)}), bf16[512,1536]{1,0:T(8,128)(2,1)}) %all-gather.7.cloned.1.call-update) | async-done | bytes 1572880 | tf_op jit(solution)/shard_map/all_gather | solution.py:109
  104.8 9.8 %fusion.53 = (f32[512]{0:T(512)S(1)}, f32[512,3072]{1,0:T(8,128)}) fusion(bf16[512,1536]{1,0:T(8,128)(2,1)} %all-gather.7.cloned.1.call-done, bf16[1536,3072]{1,0:T(8,128)(2,1)} %param.9), kind=kOutput, calls=%fused_computation.161 | convolution fusion | flops 4833410560 | bytes 17303552 | tf_op jit(solution)/shard_map/while/body/eval_jaxpr/dot_general | solution.py:74
  114.7 4.6 %fusion.1 = (f32[512]{0:T(512)S(1)}, f32[512]{0:T(512)S(1)}, f32[512]{0:T(512)S(1)}) fusion(f32[512,3072]{1,0:T(8,128)} %get-tuple-element.115, f32[512]{0:T(512)S(1)} %get-tuple-element.114, s32[512]{0:T(512)S(1)} %eq.80), kind=kLoop, calls=%fused_computation.12 | loop fusion | flops 11008512 | bytes 6301696 | tf_op jit(solution)/shard_map/while/body/eval_jaxpr/reduce_sum | solution.py:77
  119.6 30.5 %all-gather.9.cloned.1.call-done = bf16[512,1536]{1,0:T(8,128)(2,1)} async-done(((bf16[32,1536]{1,0:T(8,128)(2,1)}), bf16[512,1536]{1,0:T(8,128)(2,1)}) %all-gather.9.cloned.1.call-update) | async-done | bytes 1572880 | tf_op jit(solution)/shard_map/all_gather | solution.py:109
  150.0 9.8 %fusion.52 = (f32[512]{0:T(512)S(1)}, f32[512,3072]{1,0:T(8,128)}) fusion(bf16[512,1536]{1,0:T(8,128)(2,1)} %all-gather.9.cloned.1.call-done, bf16[1536,3072]{1,0:T(8,128)(2,1)} %param.9), kind=kOutput, calls=%fused_computation.160 | convolution fusion | flops 4833410560 | bytes 17303552 | tf_op jit(solution)/shard_map/while/body/eval_jaxpr/dot_general | solution.py:74
  160.0 4.6 %fusion = (f32[512]{0:T(512)S(1)}, f32[512]{0:T(512)S(1)}, f32[512]{0:T(512)S(1)}) fusion(f32[512,3072]{1,0:T(8,128)} %get-tuple-element.113, f32[512]{0:T(512)S(1)} %get-tuple-element.112, s32[512]{0:T(512)S(1)} %eq.84), kind=kLoop, calls=%fused_computation.7 | loop fusion | flops 11008512 | bytes 6301696 | tf_op jit(solution)/shard_map/while/body/eval_jaxpr/reduce_sum | solution.py:77
  165.0 0.1 reshape.534
  165.1 1.0 collective-permute-start
  166.1 2.4 %collective-permute-start.1 = (f32[4,1536]{1,0:T(4,128)S(1)}, f32[4,1536]{1,0:T(4,128)S(1)}, u32[]{:S(2)}, u32[]{:S(2)}) collective-permute-start(f32[4,1536]{1,0:T(4,128)S(1)} %reshape.534), channel_id=1, source_target_pairs={{0,2},{1,3},{2,0},{3,1},{4,6},{5,7},{6,4},{7,5},{8,10},{9,11},{10,... | collective-permute-start | bytes 73736 | tf_op jit(solution)/shard_map/ppermute | solution.py:54
  168.7 0.4 collective-permute-done
  169.1 1.2 collective-permute-done.1
  170.3 1.2 collective-permute-done.2
  171.5 0.6 gather_fusion.1
  172.5 1.8 collective-permute-start.4
  174.2 1.2 collective-permute-start.5
  176.2 0.2 collective-permute-done.3
  176.4 0.6 collective-permute-done.4
  176.9 0.3 collective-permute-done.5
  177.2 0.6 gather_fusion.2
  177.9 0.8 select_reduce_fusion.3
  178.8 0.7 pad_maximum_fusion.3
  179.5 5.9 %collective-permute-start.6 = (f32[2]{0:T(128)S(1)}, f32[2]{0:T(128)S(1)}, u32[]{:S(2)}, u32[]{:S(2)}) collective-permute-start(f32[2]{0:T(128)S(1)} %pad_maximum_fusion.3), channel_id=1, source_target_pairs={{0,16},{16,32},{32,48},{48,64},{64,80},{80,96},{96,112},{112,0},{1... | collective-permute-start | bytes 32 | tf_op jit(solution)/shard_map/ppermute | solution.py:54
  185.4 1.2 collective-permute-start.7
  186.6 1.5 collective-permute-start.8
  188.1 0.5 collective-permute-start.9
  188.6 2.0 collective-permute-start.10
  190.7 0.7 fusion.61
  191.5 0.2 fusion.41
  191.7 0.2 fusion.40
  191.9 0.2 select_dynamic-update-slice_fusion
  192.1 0.7 collective-permute-start.11
  192.8 1.6 collective-permute-start.12
  194.6 1.3 collective-permute-done.12
  195.9 0.6 gather_fusion
  196.5 0.6 fusion.50
  (68 shorter events, 3.2 us)
Async XLA Ops:
  7.2 52.3 %all-gather.5.cloned.1.call-start = ((), (), s32[]{:S(2)}) async-start(), calls=%async_computation | async-start | bytes 1671168 | tf_op jit(solution)/shard_map/all_gather | solution.py:109
  13.5 91.2 %all-gather.7.cloned.1.call-start = ((), (), s32[]{:S(2)}) async-start(), calls=%async_computation.1 | async-start | bytes 1671168 | tf_op jit(solution)/shard_map/all_gather | solution.py:109
  14.3 135.8 %all-gather.9.cloned.1.call-start = ((), (), s32[]{:S(2)}) async-start(), calls=%async_computation.2 | async-start | bytes 1671168 | tf_op jit(solution)/shard_map/all_gather | solution.py:109
  165.1 4.0 %collective-permute-start = (f32[4,1536]{1,0:T(4,128)S(1)}, f32[4,1536]{1,0:T(4,128)S(1)}, u32[]{:S(2)}, u32[]{:S(2)}) collective-permute-start(f32[4,1536]{1,0:T(4,128)S(1)} %reshape.534), channel_id=1, source_target_pairs={{0,1},{1,2},{2,3},{3,0},{4,5},{5,6},{6,7},{7,4},{8,9},{9,10},{10,1... | collective-permute-start | bytes 73736 | tf_op jit(solution)/shard_map/ppermute | solution.py:54
  166.1 4.2 %collective-permute-start.1 = (f32[4,1536]{1,0:T(4,128)S(1)}, f32[4,1536]{1,0:T(4,128)S(1)}, u32[]{:S(2)}, u32[]{:S(2)}) collective-permute-start(f32[4,1536]{1,0:T(4,128)S(1)} %reshape.534), channel_id=1, source_target_pairs={{0,2},{1,3},{2,0},{3,1},{4,6},{5,7},{6,4},{7,5},{8,10},{9,11},{10,... | collective-permute-start | bytes 73736 | tf_op jit(solution)/shard_map/ppermute | solution.py:54
  168.5 3.0 %collective-permute-start.2 = (f32[4,1536]{1,0:T(4,128)S(1)}, f32[4,1536]{1,0:T(4,128)S(1)}, u32[]{:S(2)}, u32[]{:S(2)}) collective-permute-start(f32[4,1536]{1,0:T(4,128)S(1)} %reshape.534), channel_id=1, source_target_pairs={{0,3},{1,0},{2,1},{3,2},{4,7},{5,4},{6,5},{7,6},{8,11},{9,8},{10,9... | collective-permute-start | bytes 73736 | tf_op jit(solution)/shard_map/ppermute | solution.py:54
  172.4 4.0 %collective-permute-start.3 = (f32[4,1536]{1,0:T(4,128)S(1)}, f32[4,1536]{1,0:T(4,128)S(1)}, u32[]{:S(2)}, u32[]{:S(2)}) collective-permute-start(f32[4,1536]{1,0:T(4,128)S(1)} %get-tuple-element.104), channel_id=1, source_target_pairs={{0,4},{1,5},{2,6},{3,7},{4,8},{5,9},{6,10},{7,11},{8,12},{9,13},{1... | collective-permute-start | bytes 73736 | tf_op jit(solution)/shard_map/ppermute | solution.py:54
  172.5 4.4 %collective-permute-start.4 = (f32[4,1536]{1,0:T(4,128)S(1)}, f32[4,1536]{1,0:T(4,128)S(1)}, u32[]{:S(2)}, u32[]{:S(2)}) collective-permute-start(f32[4,1536]{1,0:T(4,128)S(1)} %get-tuple-element.104), channel_id=1, source_target_pairs={{0,8},{1,9},{2,10},{3,11},{4,12},{5,13},{6,14},{7,15},{8,0},{9,1},... | collective-permute-start | bytes 73736 | tf_op jit(solution)/shard_map/ppermute | solution.py:54
  174.2 3.0 %collective-permute-start.5 = (f32[4,1536]{1,0:T(4,128)S(1)}, f32[4,1536]{1,0:T(4,128)S(1)}, u32[]{:S(2)}, u32[]{:S(2)}) collective-permute-start(f32[4,1536]{1,0:T(4,128)S(1)} %get-tuple-element.104), channel_id=1, source_target_pairs={{0,12},{1,13},{2,14},{3,15},{4,0},{5,1},{6,2},{7,3},{8,4},{9,5},{1... | collective-permute-start | bytes 73736 | tf_op jit(solution)/shard_map/ppermute | solution.py:54
  179.5 12.6 %collective-permute-start.6 = (f32[2]{0:T(128)S(1)}, f32[2]{0:T(128)S(1)}, u32[]{:S(2)}, u32[]{:S(2)}) collective-permute-start(f32[2]{0:T(128)S(1)} %pad_maximum_fusion.3), channel_id=1, source_target_pairs={{0,16},{16,32},{32,48},{48,64},{64,80},{80,96},{96,112},{112,0},{1... | collective-permute-start | bytes 32 | tf_op jit(solution)/shard_map/ppermute | solution.py:54
  185.4 7.4 %collective-permute-start.7 = (f32[2]{0:T(128)S(1)}, f32[2]{0:T(128)S(1)}, u32[]{:S(2)}, u32[]{:S(2)}) collective-permute-start(f32[2]{0:T(128)S(1)} %pad_maximum_fusion.3), channel_id=1, source_target_pairs={{0,32},{16,48},{32,64},{48,80},{64,96},{80,112},{96,0},{112,16},{1... | collective-permute-start | bytes 32 | tf_op jit(solution)/shard_map/ppermute | solution.py:54
  186.6 7.8 %collective-permute-start.8 = (f32[2]{0:T(128)S(1)}, f32[2]{0:T(128)S(1)}, u32[]{:S(2)}, u32[]{:S(2)}) collective-permute-start(f32[2]{0:T(128)S(1)} %pad_maximum_fusion.3), channel_id=1, source_target_pairs={{0,48},{16,64},{32,80},{48,96},{64,112},{80,0},{96,16},{112,32},{1... | collective-permute-start | bytes 32 | tf_op jit(solution)/shard_map/ppermute | solution.py:54
  188.1 6.3 %collective-permute-start.9 = (f32[2]{0:T(128)S(1)}, f32[2]{0:T(128)S(1)}, u32[]{:S(2)}, u32[]{:S(2)}) collective-permute-start(f32[2]{0:T(128)S(1)} %pad_maximum_fusion.3), channel_id=1, source_target_pairs={{0,64},{16,80},{32,96},{48,112},{64,0},{80,16},{96,32},{112,48},{1... | collective-permute-start | bytes 32 | tf_op jit(solution)/shard_map/ppermute | solution.py:54
  188.6 5.8 %collective-permute-start.10 = (f32[2]{0:T(128)S(1)}, f32[2]{0:T(128)S(1)}, u32[]{:S(2)}, u32[]{:S(2)}) collective-permute-start(f32[2]{0:T(128)S(1)} %pad_maximum_fusion.3), channel_id=1, source_target_pairs={{0,80},{16,96},{32,112},{48,0},{64,16},{80,32},{96,48},{112,64},{1... | collective-permute-start | bytes 32 | tf_op jit(solution)/shard_map/ppermute | solution.py:54
  191.7 6.9 %copy-start.1 = (f32[128]{0:T(128)}, f32[128]{0:T(128)S(1)}, u32[]{:S(2)}) copy-start(f32[128]{0:T(128)S(1)} %fusion.41) | copy-start | bytes 1540
  191.9 6.6 %copy-start.2 = (f32[128]{0:T(128)}, f32[128]{0:T(128)S(1)}, u32[]{:S(2)}) copy-start(f32[128]{0:T(128)S(1)} %fusion.40) | copy-start | bytes 1540
  192.1 6.5 %copy-start = (f32[128]{0:T(128)}, f32[128]{0:T(128)S(1)}, u32[]{:S(2)}) copy-start(f32[128]{0:T(128)S(1)} %select_dynamic-update-slice_fusion) | copy-start | bytes 1540
  192.1 2.5 %collective-permute-start.11 = (f32[2]{0:T(128)S(1)}, f32[2]{0:T(128)S(1)}, u32[]{:S(2)}, u32[]{:S(2)}) collective-permute-start(f32[2]{0:T(128)S(1)} %pad_maximum_fusion.3), channel_id=1, source_target_pairs={{0,96},{16,112},{32,0},{48,16},{64,32},{80,48},{96,64},{112,80},{1... | collective-permute-start | bytes 32 | tf_op jit(solution)/shard_map/ppermute | solution.py:54
  192.8 3.1 %collective-permute-start.12 = (f32[2]{0:T(128)S(1)}, f32[2]{0:T(128)S(1)}, u32[]{:S(2)}, u32[]{:S(2)}) collective-permute-start(f32[2]{0:T(128)S(1)} %pad_maximum_fusion.3), channel_id=1, source_target_pairs={{0,112},{16,0},{32,16},{48,32},{64,48},{80,64},{96,80},{112,96},{1... | collective-permute-start | bytes 32 | tf_op jit(solution)/shard_map/ppermute | solution.py:54
Sparse Core Ops, SparseCore 0:
  13.7 45.7 all-gather.4
  61.6 43.0 all-gather.6
  106.9 43.0 all-gather.8
where the time goes:
time: 206 us
  waiting for transfers between devices  91.6 us (44%)
  matrix products  29.5 us (14%)
  between operations  21.1 us (10%)
  other arithmetic  20.5 us (10%)
  starting transfers between devices  20.1 us (10%)
  blocking collectives  14.9 us (7%)
  local copies, waits for them, and re-layouts  8.43 us (4%)
    all_gather x3, waiting for transfers between devices, shards(): lax.all_gather(normed[first:first + CHUNK], 'voc', axis=0, tiled=True)  85.1 us
    dot_general x3, matrix products, one_block(): logits = jnp.dot(rows_in, head, preferred_element_type=jnp.float32)  29.5 us
    ppermute x13, starting transfers between devices, members(): received.append(lax.ppermute(value, axis, pairs))  20 us
    unnamed x1, blocking collectives  14.9 us
    reduce_sum x3, other arithmetic, one_block(): total = jnp.sum(expo, axis=-1)  13.9 us
    ppermute x13, waiting for transfers between devices, members(): received.append(lax.ppermute(value, axis, pairs))  5.17 us
  transfers between devices with their start and end apart: 16, of which 11 were waited for; matrix products, arithmetic and copies ran while one was open for 17% of the time, Pallas kernels for 0%

commit v1 on v0

--- a/solution.py
+++ b/solution.py
@@ -106,7 +106,12 @@
     local_ids = gathered_ids - position * shard_width
     parts = []
     for first in range(0, LIVE, CHUNK):
-        gathered = lax.all_gather(normed[first : first + CHUNK], "voc", axis=0, tiled=True)
+        gathered = jnp.concatenate(
+            lax.all_to_all(
+                jnp.stack([normed[first : first + CHUNK]] * lax.axis_size("voc")), "voc", 0, 0
+            ),
+            axis=0,
+        )
         part = shard_stats(gathered, local_ids[:, first : first + CHUNK].reshape(-1), head)
         parts.append(part.reshape(4, groups, CHUNK))
     stats = jnp.stack(parts, axis=2).reshape(4, groups * LIVE)

time: 206 us -> 149 us (0.72)
  waiting for transfers between devices: 91.6 us -> 11.6 us
  starting transfers between devices: 20.1 us -> 43.6 us
  between operations: 21.1 us -> 8.01 us
  blocking collectives: 14.9 us -> 21.4 us
  matrix products: 29.5 us -> 32.5 us
    all_gather x3 -> x0, waiting for transfers between devices: 85.1 us -> none  [shards(): lax.all_gather(normed[first:first + CHUNK], 'voc', axis=0, tiled=True)]
    all_to_all x0 -> x3, starting transfers between devices: none -> 21.3 us  [shards(): lax.all_to_all(jnp.stack([normed[first:first + CHUNK]] * lax.axis_size('v...]
    all_to_all x0 -> x3, waiting for transfers between devices: none -> 7.46 us  [shards(): lax.all_to_all(jnp.stack([normed[first:first + CHUNK]] * lax.axis_size('v...]
    unnamed x1, blocking collectives: 14.9 us -> 21.4 us
    another operation x3 -> x6, local copies, waits for them, and re-layouts: 0.01 us -> 3.91 us  [the longest x3 3.9 us: shards(): jnp.stack([normed[first:first + CHUNK]] * lax.axis_size('voc'))]
    dot_general x3, matrix products: 29.5 us -> 32.5 us  [one_block(): logits = jnp.dot(rows_in, head, preferred_element_type=jnp.float32)]
    ppermute x13, starting transfers between devices: 20 us -> 22.3 us  [members(): received.append(lax.ppermute(value, axis, pairs))]
  transfers between devices with their start and end apart: 16 -> 16, of which waited for: 11 -> 7; matrix products, arithmetic and copies ran while one was open for 17% -> 24% of each run, Pallas kernels for 0% -> 0%
where the time goes in v1:
time: 149 us; the launch traced here: 148 us
  starting transfers between devices  43.6 us (29%)
  matrix products  32.5 us (22%)
  blocking collectives  21.4 us (14%)
  other arithmetic  20.5 us (14%)
  waiting for transfers between devices  11.6 us (8%)
  local copies, waits for them, and re-layouts  10.3 us (7%)
  between operations  8.01 us (5%)
    dot_general x3, matrix products, one_block(): logits = jnp.dot(rows_in, head, preferred_element_type=jnp.float32)  32.5 us
    ppermute x13, starting transfers between devices, members(): received.append(lax.ppermute(value, axis, pairs))  22.3 us
    unnamed x1, blocking collectives  21.4 us
    all_to_all x3, starting transfers between devices, shards(): lax.all_to_all(jnp.stack([normed[first:first + CHUNK]] * lax.axis_size('v...  21.3 us
    reduce_sum x3, other arithmetic, one_block(): total = jnp.sum(expo, axis=-1)  13.9 us
    all_to_all x3, waiting for transfers between devices, shards(): lax.all_to_all(jnp.stack([normed[first:first + CHUNK]] * lax.axis_size('v...  7.46 us
    ppermute x13, waiting for transfers between devices, members(): received.append(lax.ppermute(value, axis, pairs))  4.17 us
    another operation x3, local copies, waits for them, and re-layouts, shards(): jnp.stack([normed[first:first + CHUNK]] * lax.axis_size('voc'))  3.9 us
  transfers between devices with their start and end apart: 16, of which 7 were waited for; matrix products, arithmetic and copies ran while one was open for 24% of the time, Pallas kernels for 0%

profile of v1, /device:TPU:1, one launch (start us, length us, event | category | flops | bytes accessed | tf_op | source)
XLA Modules:
  0.0 147.9 jit_solution(6996808744537609206)
XLA Ops:
  0.7 1.3 fusion.51
  3.9 1.2 fusion.3
  5.1 1.1 fusion.5
  6.3 1.3 stack.190
  7.6 8.4 %all-to-all-start = ((bf16[16,32,1536]{2,1,0:T(8,128)(2,1)}), bf16[16,32,1536]{2,1,0:T(8,128)(2,1)S(1)}, u32[]{:S(2)}, u32[]{:S(2)}) async-start(bf16[16,32,1536]{2,1,0:T(8,128)(2,1)} %stack.190), calls=%async_computation | async-start | bytes 3145728 | tf_op jit(solution)/shard_map/all_to_all | solution.py:110
  17.4 0.6 dynamic-slice.1
  18.8 21.4 %all-reduce.1 = s32[1664]{0:T(1024)S(1)} all-reduce(s32[1664]{0:T(1024)S(1)} %pad_dynamic-update-slice_fusion), channel_id=2, replica_groups=mesh['req'=8,'voc'=16] {'voc'}, use_global_device_ids=true, to_apply=%add.1 | all-reduce | flops 1664 | bytes 13312
  40.7 0.7 slice_reduce_fusion.1
  41.4 1.3 stack.196
  42.7 6.1 %all-to-all-start.1 = ((bf16[16,32,1536]{2,1,0:T(8,128)(2,1)}), bf16[16,32,1536]{2,1,0:T(8,128)(2,1)S(1)}, u32[]{:S(2)}, u32[]{:S(2)}) async-start(bf16[16,32,1536]{2,1,0:T(8,128)(2,1)} %stack.196), calls=%async_computation.1 | async-start | bytes 3145728 | tf_op jit(solution)/shard_map/all_to_all | solution.py:110
  48.9 10.7 %fusion.54 = (f32[512]{0:T(512)S(1)}, f32[512,3072]{1,0:T(8,128)}) fusion(bf16[512,1536]{1,0:T(8,128)(2,1)S(1)} %bitcast.180, bf16[1536,3072]{1,0:T(8,128)(2,1)} %param.9), kind=kOutput, calls=%fused_computation.162 | convolution fusion | flops 4833410560 | bytes 17303552 | tf_op jit(solution)/shard_map/while/body/eval_jaxpr/dot_general | solution.py:74
  59.7 4.6 %fusion.2 = (f32[512]{0:T(512)S(1)}, f32[512]{0:T(512)S(1)}, f32[512]{0:T(512)S(1)}) fusion(f32[512,3072]{1,0:T(8,128)} %get-tuple-element.117, f32[512]{0:T(512)S(1)} %get-tuple-element.116, s32[512]{0:T(512)S(1)} %eq.76), kind=kLoop, calls=%fused_computation.17 | loop fusion | flops 11008512 | bytes 6301696 | tf_op jit(solution)/shard_map/while/body/eval_jaxpr/reduce_sum | solution.py:77
  64.6 3.3 %all-to-all-done.1 = bf16[16,32,1536]{2,1,0:T(8,128)(2,1)S(1)} async-done(((bf16[16,32,1536]{2,1,0:T(8,128)(2,1)}), bf16[16,32,1536]{2,1,0:T(8,128)(2,1)S(1)}, u32[]{:S(2)}, u32[]{:S(2)}) %all-to-all-start.1) | async-done | bytes 1572896 | tf_op jit(solution)/shard_map/all_to_all | solution.py:110
  67.8 1.3 stack.202
  69.1 6.8 %all-to-all-start.2 = ((bf16[16,32,1536]{2,1,0:T(8,128)(2,1)}), bf16[16,32,1536]{2,1,0:T(8,128)(2,1)S(1)}, u32[]{:S(2)}, u32[]{:S(2)}) async-start(bf16[16,32,1536]{2,1,0:T(8,128)(2,1)} %stack.202), calls=%async_computation.2 | async-start | bytes 3145728 | tf_op jit(solution)/shard_map/all_to_all | solution.py:110
  76.0 11.0 %fusion.53 = (f32[512]{0:T(512)S(1)}, f32[512,3072]{1,0:T(8,128)}) fusion(bf16[512,1536]{1,0:T(8,128)(2,1)S(1)} %bitcast.181, bf16[1536,3072]{1,0:T(8,128)(2,1)} %param.9), kind=kOutput, calls=%fused_computation.161 | convolution fusion | flops 4833410560 | bytes 17303552 | tf_op jit(solution)/shard_map/while/body/eval_jaxpr/dot_general | solution.py:74
  87.1 4.6 %fusion.1 = (f32[512]{0:T(512)S(1)}, f32[512]{0:T(512)S(1)}, f32[512]{0:T(512)S(1)}) fusion(f32[512,3072]{1,0:T(8,128)} %get-tuple-element.115, f32[512]{0:T(512)S(1)} %get-tuple-element.114, s32[512]{0:T(512)S(1)} %eq.80), kind=kLoop, calls=%fused_computation.12 | loop fusion | flops 11008512 | bytes 6301696 | tf_op jit(solution)/shard_map/while/body/eval_jaxpr/reduce_sum | solution.py:77
  92.0 4.2 %all-to-all-done.2 = bf16[16,32,1536]{2,1,0:T(8,128)(2,1)S(1)} async-done(((bf16[16,32,1536]{2,1,0:T(8,128)(2,1)}), bf16[16,32,1536]{2,1,0:T(8,128)(2,1)S(1)}, u32[]{:S(2)}, u32[]{:S(2)}) %all-to-all-start.2) | async-done | bytes 1572896 | tf_op jit(solution)/shard_map/all_to_all | solution.py:110
  96.2 10.7 %fusion.52 = (f32[512]{0:T(512)S(1)}, f32[512,3072]{1,0:T(8,128)}) fusion(bf16[512,1536]{1,0:T(8,128)(2,1)S(1)} %bitcast.182, bf16[1536,3072]{1,0:T(8,128)(2,1)} %param.9), kind=kOutput, calls=%fused_computation.160 | convolution fusion | flops 4833410560 | bytes 17303552 | tf_op jit(solution)/shard_map/while/body/eval_jaxpr/dot_general | solution.py:74
  107.0 4.6 %fusion = (f32[512]{0:T(512)S(1)}, f32[512]{0:T(512)S(1)}, f32[512]{0:T(512)S(1)}) fusion(f32[512,3072]{1,0:T(8,128)} %get-tuple-element.113, f32[512]{0:T(512)S(1)} %get-tuple-element.112, s32[512]{0:T(512)S(1)} %eq.84), kind=kLoop, calls=%fused_computation.7 | loop fusion | flops 11008512 | bytes 6301696 | tf_op jit(solution)/shard_map/while/body/eval_jaxpr/reduce_sum | solution.py:77
  112.1 0.6 collective-permute-start
  112.7 1.7 %collective-permute-start.1 = (f32[4,1536]{1,0:T(4,128)S(1)}, f32[4,1536]{1,0:T(4,128)S(1)}, u32[]{:S(2)}, u32[]{:S(2)}) collective-permute-start(f32[4,1536]{1,0:T(4,128)S(1)} %reshape.534), channel_id=1, source_target_pairs={{0,2},{1,3},{2,0},{3,1},{4,6},{5,7},{6,4},{7,5},{8,10},{9,11},{10,... | collective-permute-start | bytes 73736 | tf_op jit(solution)/shard_map/ppermute | solution.py:54
  114.4 0.8 collective-permute-start.2
  115.3 0.7 collective-permute-done
  116.1 0.8 collective-permute-done.1
  116.9 0.2 collective-permute-done.2
  117.1 0.6 gather_fusion.1
  118.0 2.2 %collective-permute-start.3 = (f32[4,1536]{1,0:T(4,128)S(1)}, f32[4,1536]{1,0:T(4,128)S(1)}, u32[]{:S(2)}, u32[]{:S(2)}) collective-permute-start(f32[4,1536]{1,0:T(4,128)S(1)} %get-tuple-element.104), channel_id=1, source_target_pairs={{0,4},{1,5},{2,6},{3,7},{4,8},{5,9},{6,10},{7,11},{8,12},{9,13},{1... | collective-permute-start | bytes 73736 | tf_op jit(solution)/shard_map/ppermute | solution.py:54
  120.1 1.5 %collective-permute-start.4 = (f32[4,1536]{1,0:T(4,128)S(1)}, f32[4,1536]{1,0:T(4,128)S(1)}, u32[]{:S(2)}, u32[]{:S(2)}) collective-permute-start(f32[4,1536]{1,0:T(4,128)S(1)} %get-tuple-element.104), channel_id=1, source_target_pairs={{0,8},{1,9},{2,10},{3,11},{4,12},{5,13},{6,14},{7,15},{8,0},{9,1},... | collective-permute-start | bytes 73736 | tf_op jit(solution)/shard_map/ppermute | solution.py:54
  121.7 1.0 collective-permute-start.5
  123.4 0.9 collective-permute-done.4
  124.4 0.6 gather_fusion.2
  125.1 0.8 select_reduce_fusion.3
  125.9 0.7 pad_maximum_fusion.3
  126.6 6.8 %collective-permute-start.6 = (f32[2]{0:T(128)S(1)}, f32[2]{0:T(128)S(1)}, u32[]{:S(2)}, u32[]{:S(2)}) collective-permute-start(f32[2]{0:T(128)S(1)} %pad_maximum_fusion.3), channel_id=1, source_target_pairs={{0,16},{16,32},{32,48},{48,64},{64,80},{80,96},{96,112},{112,0},{1... | collective-permute-start | bytes 32 | tf_op jit(solution)/shard_map/ppermute | solution.py:54
  133.4 1.3 collective-permute-start.7
  134.7 1.6 %collective-permute-start.8 = (f32[2]{0:T(128)S(1)}, f32[2]{0:T(128)S(1)}, u32[]{:S(2)}, u32[]{:S(2)}) collective-permute-start(f32[2]{0:T(128)S(1)} %pad_maximum_fusion.3), channel_id=1, source_target_pairs={{0,48},{16,64},{32,80},{48,96},{64,112},{80,0},{96,16},{112,32},{1... | collective-permute-start | bytes 32 | tf_op jit(solution)/shard_map/ppermute | solution.py:54
  136.4 0.3 collective-permute-start.9
  136.7 2.0 %collective-permute-start.10 = (f32[2]{0:T(128)S(1)}, f32[2]{0:T(128)S(1)}, u32[]{:S(2)}, u32[]{:S(2)}) collective-permute-start(f32[2]{0:T(128)S(1)} %pad_maximum_fusion.3), channel_id=1, source_target_pairs={{0,80},{16,96},{32,112},{48,0},{64,16},{80,32},{96,48},{112,64},{1... | collective-permute-start | bytes 32 | tf_op jit(solution)/shard_map/ppermute | solution.py:54
  138.7 0.7 fusion.61
  139.5 0.2 fusion.41
  139.8 0.2 fusion.40
  139.9 0.2 select_dynamic-update-slice_fusion
  140.1 0.9 collective-permute-start.11
  141.0 1.5 %collective-permute-start.12 = (f32[2]{0:T(128)S(1)}, f32[2]{0:T(128)S(1)}, u32[]{:S(2)}, u32[]{:S(2)}) collective-permute-start(f32[2]{0:T(128)S(1)} %pad_maximum_fusion.3), channel_id=1, source_target_pairs={{0,112},{16,0},{32,16},{48,32},{64,48},{80,64},{96,80},{112,96},{1... | collective-permute-start | bytes 32 | tf_op jit(solution)/shard_map/ppermute | solution.py:54
  142.6 1.5 %collective-permute-done.12 = f32[2]{0:T(128)S(1)} collective-permute-done((f32[2]{0:T(128)S(1)}, f32[2]{0:T(128)S(1)}, u32[]{:S(2)}, u32[]{:S(2)}) %collective-permute-start.12) | collective-permute-done | bytes 40 | tf_op jit(solution)/shard_map/ppermute | solution.py:54
  144.1 0.6 gather_fusion
  144.8 0.6 fusion.50
  (72 shorter events, 3.0 us)
Async XLA Ops:
  0.6 16.8 %copy-start.4 = (u32[128]{0:T(128)S(1)}, u32[128]{0:T(128)}, u32[]{:S(2)}) copy-start(u32[128]{0:T(128)} %constant.173) | copy-start | bytes 1540
  0.6 15.4 %copy-start = (s32[128]{0:T(128)S(1)}, s32[128]{0:T(128)}, u32[]{:S(2)}) copy-start(s32[128]{0:T(128)} %param.10) | copy-start | bytes 1540
  7.6 33.9 %all-to-all-start = ((bf16[16,32,1536]{2,1,0:T(8,128)(2,1)}), bf16[16,32,1536]{2,1,0:T(8,128)(2,1)S(1)}, u32[]{:S(2)}, u32[]{:S(2)}) async-start(bf16[16,32,1536]{2,1,0:T(8,128)(2,1)} %stack.190), calls=%async_computation | async-start | bytes 3145728 | tf_op jit(solution)/shard_map/all_to_all | solution.py:110
  42.7 25.1 %all-to-all-start.1 = ((bf16[16,32,1536]{2,1,0:T(8,128)(2,1)}), bf16[16,32,1536]{2,1,0:T(8,128)(2,1)S(1)}, u32[]{:S(2)}, u32[]{:S(2)}) async-start(bf16[16,32,1536]{2,1,0:T(8,128)(2,1)} %stack.196), calls=%async_computation.1 | async-start | bytes 3145728 | tf_op jit(solution)/shard_map/all_to_all | solution.py:110
  69.1 27.0 %all-to-all-start.2 = ((bf16[16,32,1536]{2,1,0:T(8,128)(2,1)}), bf16[16,32,1536]{2,1,0:T(8,128)(2,1)S(1)}, u32[]{:S(2)}, u32[]{:S(2)}) async-start(bf16[16,32,1536]{2,1,0:T(8,128)(2,1)} %stack.202), calls=%async_computation.2 | async-start | bytes 3145728 | tf_op jit(solution)/shard_map/all_to_all | solution.py:110
  112.1 4.0 %collective-permute-start = (f32[4,1536]{1,0:T(4,128)S(1)}, f32[4,1536]{1,0:T(4,128)S(1)}, u32[]{:S(2)}, u32[]{:S(2)}) collective-permute-start(f32[4,1536]{1,0:T(4,128)S(1)} %reshape.534), channel_id=1, source_target_pairs={{0,1},{1,2},{2,3},{3,0},{4,5},{5,6},{6,7},{7,4},{8,9},{9,10},{10,1... | collective-permute-start | bytes 73736 | tf_op jit(solution)/shard_map/ppermute | solution.py:54
  112.7 4.2 %collective-permute-start.1 = (f32[4,1536]{1,0:T(4,128)S(1)}, f32[4,1536]{1,0:T(4,128)S(1)}, u32[]{:S(2)}, u32[]{:S(2)}) collective-permute-start(f32[4,1536]{1,0:T(4,128)S(1)} %reshape.534), channel_id=1, source_target_pairs={{0,2},{1,3},{2,0},{3,1},{4,6},{5,7},{6,4},{7,5},{8,10},{9,11},{10,... | collective-permute-start | bytes 73736 | tf_op jit(solution)/shard_map/ppermute | solution.py:54
  114.4 2.7 %collective-permute-start.2 = (f32[4,1536]{1,0:T(4,128)S(1)}, f32[4,1536]{1,0:T(4,128)S(1)}, u32[]{:S(2)}, u32[]{:S(2)}) collective-permute-start(f32[4,1536]{1,0:T(4,128)S(1)} %reshape.534), channel_id=1, source_target_pairs={{0,3},{1,0},{2,1},{3,2},{4,7},{5,4},{6,5},{7,6},{8,11},{9,8},{10,9... | collective-permute-start | bytes 73736 | tf_op jit(solution)/shard_map/ppermute | solution.py:54
  118.0 5.4 %collective-permute-start.3 = (f32[4,1536]{1,0:T(4,128)S(1)}, f32[4,1536]{1,0:T(4,128)S(1)}, u32[]{:S(2)}, u32[]{:S(2)}) collective-permute-start(f32[4,1536]{1,0:T(4,128)S(1)} %get-tuple-element.104), channel_id=1, source_target_pairs={{0,4},{1,5},{2,6},{3,7},{4,8},{5,9},{6,10},{7,11},{8,12},{9,13},{1... | collective-permute-start | bytes 73736 | tf_op jit(solution)/shard_map/ppermute | solution.py:54
  120.1 4.2 %collective-permute-start.4 = (f32[4,1536]{1,0:T(4,128)S(1)}, f32[4,1536]{1,0:T(4,128)S(1)}, u32[]{:S(2)}, u32[]{:S(2)}) collective-permute-start(f32[4,1536]{1,0:T(4,128)S(1)} %get-tuple-element.104), channel_id=1, source_target_pairs={{0,8},{1,9},{2,10},{3,11},{4,12},{5,13},{6,14},{7,15},{8,0},{9,1},... | collective-permute-start | bytes 73736 | tf_op jit(solution)/shard_map/ppermute | solution.py:54
  121.7 2.7 %collective-permute-start.5 = (f32[4,1536]{1,0:T(4,128)S(1)}, f32[4,1536]{1,0:T(4,128)S(1)}, u32[]{:S(2)}, u32[]{:S(2)}) collective-permute-start(f32[4,1536]{1,0:T(4,128)S(1)} %get-tuple-element.104), channel_id=1, source_target_pairs={{0,12},{1,13},{2,14},{3,15},{4,0},{5,1},{6,2},{7,3},{8,4},{9,5},{1... | collective-permute-start | bytes 73736 | tf_op jit(solution)/shard_map/ppermute | solution.py:54
  126.6 13.5 %collective-permute-start.6 = (f32[2]{0:T(128)S(1)}, f32[2]{0:T(128)S(1)}, u32[]{:S(2)}, u32[]{:S(2)}) collective-permute-start(f32[2]{0:T(128)S(1)} %pad_maximum_fusion.3), channel_id=1, source_target_pairs={{0,16},{16,32},{32,48},{48,64},{64,80},{80,96},{96,112},{112,0},{1... | collective-permute-start | bytes 32 | tf_op jit(solution)/shard_map/ppermute | solution.py:54
  133.4 7.6 %collective-permute-start.7 = (f32[2]{0:T(128)S(1)}, f32[2]{0:T(128)S(1)}, u32[]{:S(2)}, u32[]{:S(2)}) collective-permute-start(f32[2]{0:T(128)S(1)} %pad_maximum_fusion.3), channel_id=1, source_target_pairs={{0,32},{16,48},{32,64},{48,80},{64,96},{80,112},{96,0},{112,16},{1... | collective-permute-start | bytes 32 | tf_op jit(solution)/shard_map/ppermute | solution.py:54
  134.7 7.8 %collective-permute-start.8 = (f32[2]{0:T(128)S(1)}, f32[2]{0:T(128)S(1)}, u32[]{:S(2)}, u32[]{:S(2)}) collective-permute-start(f32[2]{0:T(128)S(1)} %pad_maximum_fusion.3), channel_id=1, source_target_pairs={{0,48},{16,64},{32,80},{48,96},{64,112},{80,0},{96,16},{112,32},{1... | collective-permute-start | bytes 32 | tf_op jit(solution)/shard_map/ppermute | solution.py:54
  136.4 6.2 %collective-permute-start.9 = (f32[2]{0:T(128)S(1)}, f32[2]{0:T(128)S(1)}, u32[]{:S(2)}, u32[]{:S(2)}) collective-permute-start(f32[2]{0:T(128)S(1)} %pad_maximum_fusion.3), channel_id=1, source_target_pairs={{0,64},{16,80},{32,96},{48,112},{64,0},{80,16},{96,32},{112,48},{1... | collective-permute-start | bytes 32 | tf_op jit(solution)/shard_map/ppermute | solution.py:54
  136.7 5.9 %collective-permute-start.10 = (f32[2]{0:T(128)S(1)}, f32[2]{0:T(128)S(1)}, u32[]{:S(2)}, u32[]{:S(2)}) collective-permute-start(f32[2]{0:T(128)S(1)} %pad_maximum_fusion.3), channel_id=1, source_target_pairs={{0,80},{16,96},{32,112},{48,0},{64,16},{80,32},{96,48},{112,64},{1... | collective-permute-start | bytes 32 | tf_op jit(solution)/shard_map/ppermute | solution.py:54
  139.7 7.1 %copy-start.2 = (f32[128]{0:T(128)}, f32[128]{0:T(128)S(1)}, u32[]{:S(2)}) copy-start(f32[128]{0:T(128)S(1)} %fusion.41) | copy-start | bytes 1540
  139.9 6.8 %copy-start.3 = (f32[128]{0:T(128)}, f32[128]{0:T(128)S(1)}, u32[]{:S(2)}) copy-start(f32[128]{0:T(128)S(1)} %fusion.40) | copy-start | bytes 1540
  140.1 6.7 %copy-start.1 = (f32[128]{0:T(128)}, f32[128]{0:T(128)S(1)}, u32[]{:S(2)}) copy-start(f32[128]{0:T(128)S(1)} %select_dynamic-update-slice_fusion) | copy-start | bytes 1540
  140.1 2.5 %collective-permute-start.11 = (f32[2]{0:T(128)S(1)}, f32[2]{0:T(128)S(1)}, u32[]{:S(2)}, u32[]{:S(2)}) collective-permute-start(f32[2]{0:T(128)S(1)} %pad_maximum_fusion.3), channel_id=1, source_target_pairs={{0,96},{16,112},{32,0},{48,16},{64,32},{80,48},{96,64},{112,80},{1... | collective-permute-start | bytes 32 | tf_op jit(solution)/shard_map/ppermute | solution.py:54
  141.0 3.1 %collective-permute-start.12 = (f32[2]{0:T(128)S(1)}, f32[2]{0:T(128)S(1)}, u32[]{:S(2)}, u32[]{:S(2)}) collective-permute-start(f32[2]{0:T(128)S(1)} %pad_maximum_fusion.3), channel_id=1, source_target_pairs={{0,112},{16,0},{32,16},{48,32},{64,48},{80,64},{96,80},{112,96},{1... | collective-permute-start | bytes 32 | tf_op jit(solution)/shard_map/ppermute | solution.py:54
